TPU v7x, 128 devices: a whole 4x4x4 slice. The times are simulated.
128 devices in a mesh: dp: 8 (over z, core), expert: 16 (over x, y).
Axes of the slice: x: 4, y: 4, z: 4, core: 2. Of those that a mesh axis runs over, the one named last changes fastest.
Arguments:
- residual_in: bfloat16 [8192, 2048], P(('dp', 'expert')), may hold values from -40 to 40
- attention_gain: float32 [2048], replicated, may hold values from 0.25 to 1.75
- query_weight: bfloat16 [2048, 2048], P(None, 'expert'), may hold values from -0.125 to 0.125
- key_weight: bfloat16 [2048, 2048], P(None, 'expert'), may hold values from -0.125 to 0.125
- value_weight: bfloat16 [2048, 2048], P(None, 'expert'), may hold values from -0.125 to 0.125
- output_weight: bfloat16 [2048, 2048], P('expert'), may hold values from -0.125 to 0.125
- prompt_keys: bfloat16 [24, 2048, 2048], P('dp', None, 'expert'), may hold values from -220 to 220
- prompt_values: bfloat16 [24, 2048, 2048], P('dp', None, 'expert'), may hold values from -12 to 12
- group_index: int32 [8, 32], P('dp'), may hold values from 0 to 2, never falling along the last dimension, each value on 1 to 16 neighbouring positions
- prompt_length: int32 [24], P('dp'), may hold values from 1 to 2048, 24576 in all
- own_length: int32 [256], P('dp'), may hold values from 1 to 32
- expert_gain: float32 [2048], replicated, may hold values from 0.25 to 1.75
- expert_ids: int32 [8192, 8], P(('dp', 'expert')), may hold values from 0 to 63, all different within a row; in each aligned block of 64 rows (0 to 63, 64 to 127, ...) at most 12 rows name the same one
- expert_mix: float32 [8192, 8], P(('dp', 'expert')), may hold values from 0.02 to 0.3
- gate_weight: bfloat16 [128, 2048, 512], P(('dp', 'expert')), may hold values from -0.125 to 0.125
- up_weight: bfloat16 [128, 2048, 512], P(('dp', 'expert')), may hold values from -0.125 to 0.125
- down_weight: bfloat16 [128, 512, 2048], P(('dp', 'expert')), may hold values from -0.1875 to 0.1875
Outputs:
- attention_update: bfloat16 [8192, 2048], P(('dp', 'expert'))
- expert_update: bfloat16 [8192, 2048], P(('dp', 'expert'))
Inputs may be any that keep to these rules, and one draw needn't show every extreme that they name: `group_index`: each row holds the 32 requests of one index of dp; a group's requests are consecutive, every group has 1 to 16 requests and some group exactly 16. `prompt_length`: some prompt is exactly 2048 long. `expert_ids`: a token's 8 experts differ; among the 64 rows of one device no expert is named more than 12 times, a bound that some block reaches.
All inputs are finite; a program needn't handle non-finite values. No bound on the sum of `prompt_length` on one device may be relied on, other than what follows from the above.
Results may differ from a plain program's by a relative error of at most 0.025.
The roundings to bfloat16 on the way count: a program that leaves them out, or rounds other values in their place, can miss the bound.
Values may be sent and summed in bfloat16 or wider, within the bound.
No kernel may reach another device: no remote copies, remote signals or barrier semaphores. Data moves between devices by JAX's collectives and lax.ppermute only.
A program may use at most 128 MiB of HBM per device.

v0:
```python
import jax
import jax.numpy as jnp
from jax import lax
from jax.sharding import PartitionSpec as P

HD = 128
FF = 1024
TOP = 8
GSIZE = 16
SB = 32
epsilon = 1e-06


def rms_scale(values, gain):
    widened = values.astype(jnp.float32)
    spread = jnp.mean(widened * widened, axis=-1, keepdims=True)
    return (widened * lax.rsqrt(spread + epsilon) * gain).astype(jnp.bfloat16)


def expert_block(block, gate_weight, up_weight, down_weight):
    shape_kept = block.shape
    flat = block.reshape(-1, shape_kept[-1])
    gated = jnp.dot(flat, gate_weight[0], preferred_element_type=jnp.float32)
    lifted = jnp.dot(flat, up_weight[0], preferred_element_type=jnp.float32)
    hidden = (jax.nn.silu(gated) * lifted).astype(jnp.bfloat16)
    produced = jnp.dot(hidden, down_weight[0], preferred_element_type=jnp.float32).astype(
        jnp.bfloat16
    )
    return produced.reshape(shape_kept)


def per_device(
    residual_in,
    attention_gain,
    query_weight,
    key_weight,
    value_weight,
    output_weight,
    prompt_keys,
    prompt_values,
    group_index,
    prompt_length,
    own_length,
    expert_gain,
    expert_ids,
    expert_mix,
    gate_weight,
    up_weight,
    down_weight,
):
    tok_rows, width = residual_in.shape
    local_width = query_weight.shape[1]
    heads_here = local_width // HD
    requests = group_index.shape[1]
    longest = prompt_keys.shape[1]
    groups_here = prompt_keys.shape[0]
    normed = rms_scale(residual_in, attention_gain)
    piece = lax.all_gather(normed, "expert", axis=0, tiled=True)
    query_part = jnp.dot(piece, query_weight, preferred_element_type=jnp.float32).astype(
        jnp.bfloat16
    )
    key_part = jnp.dot(piece, key_weight, preferred_element_type=jnp.float32).astype(jnp.bfloat16)
    value_part = jnp.dot(piece, value_weight, preferred_element_type=jnp.float32).astype(
        jnp.bfloat16
    )
    projected = jnp.concatenate([query_part, key_part, value_part], axis=1)
    layout = (requests, SB, heads_here, HD)
    queries = projected[:, :local_width].reshape(layout)
    new_keys = projected[:, local_width : 2 * local_width].reshape(layout)
    new_values = projected[:, 2 * local_width :].reshape(layout)
    scale = HD ** (-0.5)
    positions = jnp.arange(SB, dtype=jnp.int32)
    own_scores = (
        jnp.einsum("rihd,rjhd->rhij", queries, new_keys, preferred_element_type=jnp.float32) * scale
    )
    own_scores = jnp.where(
        positions[None, None, None, :] < own_length[:, None, None, None], own_scores, -jnp.inf
    )
    member = group_index[0]
    prompt_positions = jnp.arange(longest, dtype=jnp.int32)

    def group_step(group, attended):
        first = jnp.sum((member < group).astype(jnp.int32))
        start = jnp.minimum(first, requests - GSIZE)
        window_queries = lax.dynamic_slice_in_dim(queries, start, GSIZE, 0)
        group_keys = lax.dynamic_index_in_dim(prompt_keys, group, 0, keepdims=False).reshape(
            longest, heads_here, HD
        )
        group_values = lax.dynamic_index_in_dim(prompt_values, group, 0, keepdims=False).reshape(
            longest, heads_here, HD
        )
        scores = (
            jnp.einsum(
                "rihd,jhd->rhij", window_queries, group_keys, preferred_element_type=jnp.float32
            )
            * scale
        )
        limit = lax.dynamic_index_in_dim(prompt_length, group, 0, keepdims=False)
        scores = jnp.where(prompt_positions < limit, scores, -jnp.inf)
        window_own = lax.dynamic_slice_in_dim(own_scores, start, GSIZE, 0)
        highest = jnp.maximum(jnp.max(scores, axis=-1), jnp.max(window_own, axis=-1))
        prompt_weights = jnp.exp(scores - highest[..., None]).astype(jnp.bfloat16)
        own_weights = jnp.exp(window_own - highest[..., None]).astype(jnp.bfloat16)
        window_values = lax.dynamic_slice_in_dim(new_values, start, GSIZE, 0)
        summed = jnp.einsum(
            "rhij,jhd->rihd", prompt_weights, group_values, preferred_element_type=jnp.float32
        )
        summed = summed + jnp.einsum(
            "rhij,rjhd->rihd", own_weights, window_values, preferred_element_type=jnp.float32
        )
        totals = jnp.sum(prompt_weights, axis=-1, dtype=jnp.float32) + jnp.sum(
            own_weights, axis=-1, dtype=jnp.float32
        )
        result = (summed / jnp.transpose(totals, (0, 2, 1))[..., None]).astype(jnp.bfloat16)
        inside = lax.dynamic_slice_in_dim(member, start, GSIZE, 0) == group
        current = lax.dynamic_slice_in_dim(attended, start, GSIZE, 0)
        merged = jnp.where(inside[:, None, None, None], result, current)
        return lax.dynamic_update_slice_in_dim(attended, merged, start, 0)

    attended = lax.fori_loop(0, groups_here, group_step, jnp.zeros(layout, jnp.bfloat16))
    flat_attended = attended.reshape(requests * SB, local_width)
    piece = flat_attended
    expert_groups = lax.axis_size("expert")
    projected_out = jnp.dot(piece, output_weight, preferred_element_type=jnp.float32).astype(
        jnp.bfloat16
    )
    partials = lax.all_to_all(
        projected_out.reshape(expert_groups, tok_rows, width), "expert", 0, 0, tiled=True
    )
    attention_update = jnp.sum(partials.astype(jnp.float32), axis=0).astype(jnp.bfloat16)
    expert_input = rms_scale(
        residual_in.astype(jnp.float32) + attention_update.astype(jnp.float32), expert_gain
    )
    data_groups = lax.axis_size("dp")
    devices = data_groups * expert_groups
    hidden_split = FF // gate_weight.shape[2]
    experts = devices // hidden_split
    capacity = max(2, tok_rows * TOP * 3 // (2 * experts))
    chosen = expert_ids.reshape(-1)
    routes_here = chosen.shape[0]
    owners = jnp.arange(routes_here, dtype=jnp.int32) // TOP
    matches = (chosen[:, None] == jnp.arange(experts, dtype=jnp.int32)[None, :]).astype(jnp.int32)
    slots = jnp.sum((jnp.cumsum(matches, axis=0) - matches) * matches, axis=1)
    table = (
        jnp.full((experts * capacity,), tok_rows, jnp.int32)
        .at[chosen * capacity + slots]
        .set(owners)
    )
    lanes = 128
    sub = width // lanes
    tiles = expert_input.reshape(tok_rows, sub, lanes)
    padded = jnp.concatenate([tiles, jnp.zeros((1, sub, lanes), jnp.bfloat16)], axis=0)
    index = jnp.broadcast_to(
        table.reshape(experts, 1, capacity), (experts, hidden_split, capacity)
    ).reshape(-1)
    outgoing = padded[index].reshape(devices, capacity * sub, lanes)
    arrived = lax.all_to_all(outgoing, ("dp", "expert"), 0, 0, tiled=True)
    produced = expert_block(
        arrived.reshape(devices * capacity, width), gate_weight, up_weight, down_weight
    )
    returned = lax.all_to_all(
        produced.reshape(devices, capacity * sub, lanes), ("dp", "expert"), 0, 0, tiled=True
    )
    pieces = returned.reshape(experts, hidden_split, capacity, sub, lanes)[chosen, :, slots]
    blended = jnp.sum(pieces.astype(jnp.float32), axis=1) * expert_mix.reshape(-1)[:, None, None]
    expert_update = (
        jnp.sum(blended.reshape(tok_rows, TOP, sub, lanes), axis=1)
        .reshape(tok_rows, width)
        .astype(jnp.bfloat16)
    )
    return (attention_update, expert_update)


def solution(mesh):
    in_specs = (
        P(("dp", "expert"), None),
        P(),
        P(None, "expert"),
        P(None, "expert"),
        P(None, "expert"),
        P("expert", None),
        P("dp", None, "expert"),
        P("dp", None, "expert"),
        P("dp", None),
        P("dp"),
        P("dp"),
        P(),
        P(("dp", "expert"), None),
        P(("dp", "expert"), None),
        P(("dp", "expert"), None, None),
        P(("dp", "expert"), None, None),
        P(("dp", "expert"), None, None),
    )
    out_specs = (P(("dp", "expert"), None), P(("dp", "expert"), None))
    return jax.shard_map(
        per_device, mesh=mesh, in_specs=in_specs, out_specs=out_specs, check_vma=False
    )
```

profile of v0, /device:TPU:1, one launch (start us, length us, event | category | flops | bytes accessed | tf_op | source)
XLA Modules:
  0.0 408.5 jit_solution(3782199950880802426)
XLA Ops:
  11.1 54.0 %all-gather.2.cloned.1.call-done = bf16[1024,2048]{1,0:T(8,128)(2,1)} async-done(((bf16[64,2048]{1,0:T(8,128)(2,1)}), bf16[1024,2048]{1,0:T(8,128)(2,1)}) %all-gather.2.cloned.1.call-update) | async-done | bytes 4194320 | tf_op jit(solution)/shard_map/all_gather | solution.py:58
  65.1 3.7 convolution_convert_fusion.4
  71.7 24.7 %while.14 = (s32[]{:T(128)}, bf16[32,32,1,128]{3,1,0,2:T(8,128)(2,1)S(1)}, s32[32]{0:T(128)S(1)}, bf16[3,2048,128]{2,1,0:T(8,128)(2,1)}, s32[3]{0:T(128)S(1)}, /...) while((s32[]{:T(128)}, ...), condition=%wide.region_7.8_spmd.clone, body=%wide.region_1.7_spmd.clone.sunk | while | flops 555074688 | bytes 15133611 | solution.py:120
  74.2 1.9 bitcast_reduce_fusion.2
  77.8 2.1 fusion.93
  82.4 1.9 bitcast_reduce_fusion.2
  86.0 2.1 fusion.93
  90.6 1.9 bitcast_reduce_fusion.2
  94.3 2.1 fusion.93
  96.3 4.3 %convolution_convert_fusion.1 = bf16[1024,2048]{1,0:T(8,128)(2,1)} fusion(bf16[1024,128]{1,0:T(8,128)(2,1)S(1)} %bitcast.178, bf16[128,2048]{1,0:T(8,128)(2,1)} %param.24), kind=kOutput, calls=%fused_computation.44 | convolution fusion | flops 538968064 | bytes 4980736 | tf_op jit(solution)/shard_map/dot_general | solution.py:124
  100.6 5.2 %all-to-all-start = ((bf16[16,64,2048]{2,1,0:T(8,128)(2,1)}), bf16[16,64,2048]{2,1,0:T(8,128)(2,1)}, u32[]{:S(2)}, u32[]{:S(2)}) async-start(bf16[16,64,2048]{2,1,0:T(8,128)(2,1)} %bitcast.174), calls=%async_computation | async-start | bytes 8388608 | tf_op jit(solution)/shard_map/all_to_all | solution.py:127
  107.8 2.4 scatter_custom_fusion
  110.6 54.0 %all-to-all-done = bf16[16,64,2048]{2,1,0:T(8,128)(2,1)} async-done(((bf16[16,64,2048]{2,1,0:T(8,128)(2,1)}), bf16[16,64,2048]{2,1,0:T(8,128)(2,1)}, u32[]{:S(2)}, u32[]{:S(2)}) %all-to-all-start) | async-done | bytes 4194336 | tf_op jit(solution)/shard_map/all_to_all | solution.py:127
  164.6 3.0 reduce_sum.97
  168.0 5.7 %gather_fusion = bf16[1536,16,128]{2,1,0:T(8,128)(2,1)} fusion(bf16[65,16,128]{2,1,0:T(8,128)(2,1)S(1)} %concatenate.6, s32[2048]{0:T(1024)S(1)} %pad_clamp_fusion), kind=kCustom, calls=%fused_computation | custom fusion | bytes 12589056 | tf_op jit(solution)/shard_map/gather | solution.py:156
  173.8 91.0 %all_to_all.15 = bf16[128,192,128]{2,1,0:T(8,128)(2,1)} all-to-all(bf16[128,192,128]{2,1,0:T(8,128)(2,1)} %bitcast.175), channel_id=1, replica_groups=mesh['dp'=8,'expert'=16] {'dp','expert'}, dimensions={0} | all-to-all | bytes 12582912 | tf_op jit(solution)/shard_map/all_to_all | solution.py:157
  264.7 10.3 %reshape.320 = bf16[1536,2048]{1,0:T(8,128)(2,1)} reshape(bf16[128,192,128]{2,1,0:T(8,128)(2,1)} %all_to_all.15) | data formatting | bytes 12582912 | tf_op jit(solution)/shard_map/reshape | solution.py:159
  275.0 8.5 %fusion.44 = f32[1536,512]{1,0:T(8,128)} fusion(bf16[1536,2048]{1,0:T(8,128)(2,1)} %reshape.320, bf16[1,2048,512]{2,1,0:T(8,128)(2,1)} %param.33), kind=kOutput, calls=%fused_computation.49 | convolution fusion | flops 3221225472 | bytes 11534336 | tf_op jit(solution)/shard_map/dot_general | solution.py:23
  283.6 11.7 %convolution_convert_fusion = bf16[1536,2048]{1,0:T(8,128)(2,1)} fusion(bf16[1,512,2048]{2,1,0:T(8,128)(2,1)S(1)} %copy-done, bf16[1536,2048]{1,0:T(8,128)(2,1)} %reshape.320, f32[1536,512]{1,0:T(8,128)} %fusion.44, bf16[1,2048,512]{2,1,0:T(8,128)(2,1)} %param.34), kind=kOutput, calls=%fused_computation.42 | convolution fusion | flops 6450315264 | bytes 19922944 | tf_op jit(solution)/shard_map/dot_general | solution.py:26
  295.3 10.5 %reshape.321 = bf16[128,192,128]{2,1,0:T(8,128)(2,1)} reshape(bf16[1536,2048]{1,0:T(8,128)(2,1)} %convolution_convert_fusion) | data formatting | bytes 12582912 | tf_op jit(solution)/shard_map/reshape | solution.py:162
  305.8 5.6 %all-to-all-start.2 = ((bf16[128,192,128]{2,1,0:T(8,128)(2,1)}), bf16[128,192,128]{2,1,0:T(8,128)(2,1)}, u32[]{:S(2)}, u32[]{:S(2)}) async-start(bf16[128,192,128]{2,1,0:T(8,128)(2,1)} %reshape.321), calls=%async_computation.2 | async-start | bytes 12582912 | tf_op jit(solution)/shard_map/all_to_all | solution.py:161
  311.5 75.4 %all-to-all-done.2 = bf16[128,192,128]{2,1,0:T(8,128)(2,1)} async-done(((bf16[128,192,128]{2,1,0:T(8,128)(2,1)}), bf16[128,192,128]{2,1,0:T(8,128)(2,1)}, u32[]{:S(2)}, u32[]{:S(2)}) %all-to-all-start.2) | async-done | bytes 6291488 | tf_op jit(solution)/shard_map/all_to_all | solution.py:161
  386.9 8.9 %gather_fusion.1 = bf16[512,2,16,128]{3,2,1,0:T(8,128)(2,1)} fusion(bf16[64,2,12,16,128]{4,3,2,1,0:T(8,128)(2,1)} %bitcast.15, s32[512]{0:T(512)S(1)} %bitcast.173), kind=kCustom, calls=%fused_computation.1 | custom fusion | bytes 8392704 | tf_op jit(solution)/shard_map/gather | solution.py:164
  395.8 4.1 %convert_reduce_fusion.2 = f32[512,16,128]{2,1,0:T(8,128)S(1)} fusion(bf16[512,2,16,128]{3,2,1,0:T(8,128)(2,1)} %gather_fusion.1), kind=kLoop, calls=%fused_computation.41 | loop fusion | flops 3145728 | bytes 8388608 | tf_op jit(solution)/shard_map/reduce_sum | solution.py:165
  (87 shorter events, 21.9 us)
Async XLA Ops:
  7.2 276.4 %copy-start = (bf16[1,512,2048]{2,1,0:T(8,128)(2,1)S(1)}, bf16[1,512,2048]{2,1,0:T(8,128)(2,1)}, u32[]{:S(2)}) copy-start(bf16[1,512,2048]{2,1,0:T(8,128)(2,1)} %param.35) | copy-start | bytes 6291460
  7.2 61.6 %copy-start.8 = (bf16[2048,128]{1,0:T(8,128)(2,1)S(1)}, bf16[2048,128]{1,0:T(8,128)(2,1)}, u32[]{:S(2)}) copy-start(bf16[2048,128]{1,0:T(8,128)(2,1)} %param.22) | copy-start | bytes 1572868
  7.2 57.9 %all-gather.2.cloned.1.call-start = ((), (), s32[]{:S(2)}) async-start(), calls=%async_computation.3 | async-start | bytes 4456448 | tf_op jit(solution)/shard_map/all_gather | solution.py:58
  65.1 3.7 copy-start.7
  68.8 1.6 copy-start.9
  70.0 1.6 copy-start.3
  70.1 1.6 copy-start.10
  100.6 5.2 %copy-start.5 = (s32[64,8]{0,1:T(8,128)S(1)}, s32[64,8]{0,1:T(8,128)}, u32[]{:S(2)}) copy-start(s32[64,8]{0,1:T(8,128)} %param.31) | copy-start | bytes 6148
  100.6 64.0 %all-to-all-start = ((bf16[16,64,2048]{2,1,0:T(8,128)(2,1)}), bf16[16,64,2048]{2,1,0:T(8,128)(2,1)}, u32[]{:S(2)}, u32[]{:S(2)}) async-start(bf16[16,64,2048]{2,1,0:T(8,128)(2,1)} %bitcast.174), calls=%async_computation | async-start | bytes 8388608 | tf_op jit(solution)/shard_map/all_to_all | solution.py:127
  105.8 61.8 %copy-start.1 = (bf16[64,2048]{1,0:T(8,128)(2,1)S(1)}, bf16[64,2048]{1,0:T(8,128)(2,1)}, u32[]{:S(2)}) copy-start(bf16[64,2048]{1,0:T(8,128)(2,1)} %param.19) | copy-start | bytes 786436
  105.8 62.0 %copy-start.4 = (f32[2048]{0:T(1024)S(1)}, f32[2048]{0:T(1024)}, u32[]{:S(2)}) copy-start(f32[2048]{0:T(1024)} %param.30) | copy-start | bytes 24580
  167.6 6.1 %copy-start.2 = (bf16[64,2048]{1,0:T(8,128)(2,1)}, bf16[64,2048]{1,0:T(8,128)(2,1)S(1)}, u32[]{:S(2)}) copy-start(bf16[64,2048]{1,0:T(8,128)(2,1)S(1)} %reduce_sum.97) | copy-start | bytes 786436
  305.8 5.6 %copy-start.6 = (f32[64,8]{0,1:T(8,128)S(1)}, f32[64,8]{0,1:T(8,128)}, u32[]{:S(2)}) copy-start(f32[64,8]{0,1:T(8,128)} %param.32) | copy-start | bytes 6148
  305.8 81.2 %all-to-all-start.2 = ((bf16[128,192,128]{2,1,0:T(8,128)(2,1)}), bf16[128,192,128]{2,1,0:T(8,128)(2,1)}, u32[]{:S(2)}, u32[]{:S(2)}) async-start(bf16[128,192,128]{2,1,0:T(8,128)(2,1)} %reshape.321), calls=%async_computation.2 | async-start | bytes 12582912 | tf_op jit(solution)/shard_map/all_to_all | solution.py:161
Sparse Core Ops, SparseCore 0:
  10.7 54.2 all-gather.1
where the time goes:
time: 410 us; the launch traced here: 408 us
  waiting for transfers between devices  183 us (45%)
  blocking collectives  91 us (22%)
  matrix products  43.5 us (11%)
  local copies, waits for them, and re-layouts  41.5 us (10%)
  other arithmetic  21.8 us (5%)
  between operations  14.3 us (3%)
  starting transfers between devices  10.8 us (3%)
    all_to_all x1, blocking collectives, per_device(): arrived = lax.all_to_all(outgoing, ('dp', 'expert'), 0, 0, tiled=True)  91 us
    all_to_all x1, waiting for transfers between devices, per_device(): lax.all_to_all(produced.reshape(devices, capacity * sub, lanes), ('dp', '...  75.4 us
    all_to_all x1, waiting for transfers between devices, per_device(): lax.all_to_all(projected_out.reshape(expert_groups, tok_rows, width), 'ex...  54 us
    all_gather x1, waiting for transfers between devices, per_device(): piece = lax.all_gather(normed, 'expert', axis=0, tiled=True)  54 us
    dot_general x1, matrix products, expert_block(): jnp.dot(hidden, down_weight[0], preferred_element_type=jnp.float32)  11.7 us
    reshape x1, local copies, waits for them, and re-layouts, per_device(): produced.reshape(devices, capacity * sub, lanes)  10.5 us
    reshape x1, local copies, waits for them, and re-layouts, per_device(): arrived.reshape(devices * capacity, width)  10.3 us
    gather x1, local copies, waits for them, and re-layouts, per_device(): returned.reshape(experts, hidden_split, capacity, sub, lanes)  8.94 us
  transfers between devices with their start and end apart: 3, of which 3 were waited for; matrix products, arithmetic and copies ran while one was open for 1% of the time, Pallas kernels for 0%

commit v1 on v0

--- a/solution.py
+++ b/solution.py
@@ -55,7 +55,9 @@
     longest = prompt_keys.shape[1]
     groups_here = prompt_keys.shape[0]
     normed = rms_scale(residual_in, attention_gain)
-    piece = lax.all_gather(normed, "expert", axis=0, tiled=True)
+    piece = jnp.concatenate(
+        lax.all_to_all(jnp.stack([normed] * lax.axis_size("expert")), "expert", 0, 0), axis=0
+    )
     query_part = jnp.dot(piece, query_weight, preferred_element_type=jnp.float32).astype(
         jnp.bfloat16
     )

time: 410 us -> 411 us (level)
  starting transfers between devices: 10.8 us -> 25 us
  between operations: 14.3 us -> 0.94 us
  matrix products: 43.5 us -> 47.8 us
    all_to_all x0 -> x1, waiting for transfers between devices: none -> 60.2 us  [per_device(): lax.all_to_all(jnp.stack([normed] * lax.axis_size('expert')), 'expert', 0...]
    all_gather x1 -> x0, waiting for transfers between devices: 54 us -> none  [per_device(): piece = lax.all_gather(normed, 'expert', axis=0, tiled=True)]
    all_to_all x0 -> x1, starting transfers between devices: none -> 7.76 us  [per_device(): lax.all_to_all(jnp.stack([normed] * lax.axis_size('expert')), 'expert', 0...]
    all_to_all x1, waiting for transfers between devices: 54 us -> 46.6 us  [per_device(): lax.all_to_all(projected_out.reshape(expert_groups, tok_rows, width), 'ex...]
    all_to_all x1, starting transfers between devices: 5.17 us -> 11.6 us  [per_device(): lax.all_to_all(projected_out.reshape(expert_groups, tok_rows, width), 'ex...]
where the time goes in v1:
time: 411 us; the launch traced here: 410 us
  waiting for transfers between devices  182 us (44%)
  blocking collectives  87.2 us (21%)
  matrix products  47.8 us (12%)
  local copies, waits for them, and re-layouts  44 us (11%)
  starting transfers between devices  25 us (6%)
  other arithmetic  20.4 us (5%)
    all_to_all x1, blocking collectives, per_device(): arrived = lax.all_to_all(outgoing, ('dp', 'expert'), 0, 0, tiled=True)  87.2 us
    all_to_all x1, waiting for transfers between devices, per_device(): lax.all_to_all(produced.reshape(devices, capacity * sub, lanes), ('dp', '...  75.4 us
    all_to_all x1, waiting for transfers between devices, per_device(): lax.all_to_all(jnp.stack([normed] * lax.axis_size('expert')), 'expert', 0...  60.2 us
    all_to_all x1, waiting for transfers between devices, per_device(): lax.all_to_all(projected_out.reshape(expert_groups, tok_rows, width), 'ex...  46.6 us
    dot_general x1, matrix products, expert_block(): jnp.dot(hidden, down_weight[0], preferred_element_type=jnp.float32)  11.7 us
    all_to_all x1, starting transfers between devices, per_device(): lax.all_to_all(projected_out.reshape(expert_groups, tok_rows, width), 'ex...  11.6 us
    reshape x1, local copies, waits for them, and re-layouts, per_device(): produced.reshape(devices, capacity * sub, lanes)  10.5 us
    reshape x1, local copies, waits for them, and re-layouts, per_device(): arrived.reshape(devices * capacity, width)  10.3 us
  transfers between devices with their start and end apart: 3, of which 3 were waited for; matrix products, arithmetic and copies ran while one was open for 1% of the time, Pallas kernels for 0%

profile of v1, /device:TPU:1, one launch (start us, length us, event | category | flops | bytes accessed | tf_op | source)
XLA Modules:
  0.0 409.8 jit_solution(16017133245089518491)
XLA Ops:
  3.0 2.5 stack.2
  5.5 7.8 %all-to-all-start = ((bf16[16,64,2048]{2,1,0:T(8,128)(2,1)}), bf16[16,64,2048]{2,1,0:T(8,128)(2,1)}, u32[]{:S(2)}, u32[]{:S(2)}) async-start(bf16[16,64,2048]{2,1,0:T(8,128)(2,1)} %stack.2), calls=%async_computation | async-start | bytes 8388608 | tf_op jit(solution)/shard_map/all_to_all | solution.py:59
  13.4 60.2 %all-to-all-done = bf16[16,64,2048]{2,1,0:T(8,128)(2,1)} async-done(((bf16[16,64,2048]{2,1,0:T(8,128)(2,1)}), bf16[16,64,2048]{2,1,0:T(8,128)(2,1)}, u32[]{:S(2)}, u32[]{:S(2)}) %all-to-all-start) | async-done | bytes 4194336 | tf_op jit(solution)/shard_map/all_to_all | solution.py:59
  73.6 3.4 convolution_convert_fusion.4
  77.0 3.6 convolution_convert_fusion.3
  80.7 3.4 convolution_convert_fusion.2
  84.5 24.7 %while.14 = (s32[]{:T(128)}, bf16[32,32,1,128]{3,1,0,2:T(8,128)(2,1)S(1)}, s32[32]{0:T(128)S(1)}, bf16[3,2048,128]{2,1,0:T(8,128)(2,1)}, s32[3]{0:T(128)S(1)}, /...) while((s32[]{:T(128)}, ...), condition=%wide.region_7.8_spmd.clone, body=%wide.region_1.7_spmd.clone.sunk | while | flops 555074688 | bytes 15133611 | solution.py:122
  98.8 2.1 fusion.93
  107.1 2.1 fusion.93
  109.1 4.3 %convolution_convert_fusion.1 = bf16[1024,2048]{1,0:T(8,128)(2,1)} fusion(bf16[1024,128]{1,0:T(8,128)(2,1)S(1)} %bitcast.179, bf16[128,2048]{1,0:T(8,128)(2,1)} %param.24), kind=kOutput, calls=%fused_computation.44 | convolution fusion | flops 538968064 | bytes 4980736 | tf_op jit(solution)/shard_map/dot_general | solution.py:126
  113.4 11.6 %all-to-all-start.1 = ((bf16[16,64,2048]{2,1,0:T(8,128)(2,1)}), bf16[16,64,2048]{2,1,0:T(8,128)(2,1)}, u32[]{:S(2)}, u32[]{:S(2)}) async-start(bf16[16,64,2048]{2,1,0:T(8,128)(2,1)} %bitcast.175), calls=%async_computation.1 | async-start | bytes 8388608 | tf_op jit(solution)/shard_map/all_to_all | solution.py:129
  127.0 2.4 scatter_custom_fusion
  129.8 46.6 %all-to-all-done.1 = bf16[16,64,2048]{2,1,0:T(8,128)(2,1)} async-done(((bf16[16,64,2048]{2,1,0:T(8,128)(2,1)}), bf16[16,64,2048]{2,1,0:T(8,128)(2,1)}, u32[]{:S(2)}, u32[]{:S(2)}) %all-to-all-start.1) | async-done | bytes 4194336 | tf_op jit(solution)/shard_map/all_to_all | solution.py:129
  176.4 3.0 reduce_sum.97
  179.8 5.7 %gather_fusion = bf16[1536,16,128]{2,1,0:T(8,128)(2,1)} fusion(bf16[65,16,128]{2,1,0:T(8,128)(2,1)S(1)} %concatenate.6, s32[2048]{0:T(1024)S(1)} %pad_clamp_fusion), kind=kCustom, calls=%fused_computation | custom fusion | bytes 12589056 | tf_op jit(solution)/shard_map/gather | solution.py:158
  185.6 87.2 %all_to_all.20 = bf16[128,192,128]{2,1,0:T(8,128)(2,1)} all-to-all(bf16[128,192,128]{2,1,0:T(8,128)(2,1)} %bitcast.176), channel_id=1, replica_groups=mesh['dp'=8,'expert'=16] {'dp','expert'}, dimensions={0} | all-to-all | bytes 12582912 | tf_op jit(solution)/shard_map/all_to_all | solution.py:159
  272.8 10.3 %reshape.326 = bf16[1536,2048]{1,0:T(8,128)(2,1)} reshape(bf16[128,192,128]{2,1,0:T(8,128)(2,1)} %all_to_all.20) | data formatting | bytes 12582912 | tf_op jit(solution)/shard_map/reshape | solution.py:161
  283.1 8.5 %fusion.44 = f32[1536,512]{1,0:T(8,128)} fusion(bf16[1536,2048]{1,0:T(8,128)(2,1)} %reshape.326, bf16[1,2048,512]{2,1,0:T(8,128)(2,1)} %param.33), kind=kOutput, calls=%fused_computation.49 | convolution fusion | flops 3221225472 | bytes 11534336 | tf_op jit(solution)/shard_map/dot_general | solution.py:23
  291.6 11.7 %convolution_convert_fusion = bf16[1536,2048]{1,0:T(8,128)(2,1)} fusion(bf16[1,512,2048]{2,1,0:T(8,128)(2,1)S(1)} %copy-done, bf16[1536,2048]{1,0:T(8,128)(2,1)} %reshape.326, f32[1536,512]{1,0:T(8,128)} %fusion.44, bf16[1,2048,512]{2,1,0:T(8,128)(2,1)} %param.34), kind=kOutput, calls=%fused_computation.42 | convolution fusion | flops 6450315264 | bytes 19922944 | tf_op jit(solution)/shard_map/dot_general | solution.py:26
  303.4 10.5 %reshape.327 = bf16[128,192,128]{2,1,0:T(8,128)(2,1)} reshape(bf16[1536,2048]{1,0:T(8,128)(2,1)} %convolution_convert_fusion) | data formatting | bytes 12582912 | tf_op jit(solution)/shard_map/reshape | solution.py:164
  313.8 5.7 %all-to-all-start.3 = ((bf16[128,192,128]{2,1,0:T(8,128)(2,1)}), bf16[128,192,128]{2,1,0:T(8,128)(2,1)}, u32[]{:S(2)}, u32[]{:S(2)}) async-start(bf16[128,192,128]{2,1,0:T(8,128)(2,1)} %reshape.327), calls=%async_computation.3 | async-start | bytes 12582912 | tf_op jit(solution)/shard_map/all_to_all | solution.py:163
  319.6 75.4 %all-to-all-done.3 = bf16[128,192,128]{2,1,0:T(8,128)(2,1)} async-done(((bf16[128,192,128]{2,1,0:T(8,128)(2,1)}), bf16[128,192,128]{2,1,0:T(8,128)(2,1)}, u32[]{:S(2)}, u32[]{:S(2)}) %all-to-all-start.3) | async-done | bytes 6291488 | tf_op jit(solution)/shard_map/all_to_all | solution.py:163
  395.0 8.9 %gather_fusion.1 = bf16[512,2,16,128]{3,2,1,0:T(8,128)(2,1)} fusion(bf16[64,2,12,16,128]{4,3,2,1,0:T(8,128)(2,1)} %bitcast.16, s32[512]{0:T(512)S(1)} %bitcast.174), kind=kCustom, calls=%fused_computation.1 | custom fusion | bytes 8392704 | tf_op jit(solution)/shard_map/gather | solution.py:166
  404.0 4.1 %convert_reduce_fusion.2 = f32[512,16,128]{2,1,0:T(8,128)S(1)} fusion(bf16[512,2,16,128]{3,2,1,0:T(8,128)(2,1)} %gather_fusion.1), kind=kLoop, calls=%fused_computation.41 | loop fusion | flops 3145728 | bytes 8388608 | tf_op jit(solution)/shard_map/reduce_sum | solution.py:167
  (87 shorter events, 25.6 us)
Async XLA Ops:
  0.6 291.0 %copy-start = (bf16[1,512,2048]{2,1,0:T(8,128)(2,1)S(1)}, bf16[1,512,2048]{2,1,0:T(8,128)(2,1)}, u32[]{:S(2)}) copy-start(bf16[1,512,2048]{2,1,0:T(8,128)(2,1)} %param.35) | copy-start | bytes 6291460
  5.5 7.8 %copy-start.7 = (s32[32]{0:T(128)S(1)}, s32[32]{0:T(128)}, u32[]{:S(2)}) copy-start(s32[32]{0:T(128)} %param.29) | copy-start | bytes 388
  5.5 68.1 %copy-start.8 = (bf16[2048,128]{1,0:T(8,128)(2,1)S(1)}, bf16[2048,128]{1,0:T(8,128)(2,1)}, u32[]{:S(2)}) copy-start(bf16[2048,128]{1,0:T(8,128)(2,1)} %param.21) | copy-start | bytes 1572868
  5.5 68.1 %all-to-all-start = ((bf16[16,64,2048]{2,1,0:T(8,128)(2,1)}), bf16[16,64,2048]{2,1,0:T(8,128)(2,1)}, u32[]{:S(2)}, u32[]{:S(2)}) async-start(bf16[16,64,2048]{2,1,0:T(8,128)(2,1)} %stack.2), calls=%async_computation | async-start | bytes 8388608 | tf_op jit(solution)/shard_map/all_to_all | solution.py:59
  77.0 3.6 copy-start.9
  80.7 3.8 copy-start.3
  80.7 3.8 copy-start.10
  113.4 11.6 %copy-start.5 = (s32[64,8]{0,1:T(8,128)S(1)}, s32[64,8]{0,1:T(8,128)}, u32[]{:S(2)}) copy-start(s32[64,8]{0,1:T(8,128)} %param.31) | copy-start | bytes 6148
  113.4 63.0 %all-to-all-start.1 = ((bf16[16,64,2048]{2,1,0:T(8,128)(2,1)}), bf16[16,64,2048]{2,1,0:T(8,128)(2,1)}, u32[]{:S(2)}, u32[]{:S(2)}) async-start(bf16[16,64,2048]{2,1,0:T(8,128)(2,1)} %bitcast.175), calls=%async_computation.1 | async-start | bytes 8388608 | tf_op jit(solution)/shard_map/all_to_all | solution.py:129
  125.0 54.4 %copy-start.1 = (bf16[64,2048]{1,0:T(8,128)(2,1)S(1)}, bf16[64,2048]{1,0:T(8,128)(2,1)}, u32[]{:S(2)}) copy-start(bf16[64,2048]{1,0:T(8,128)(2,1)} %param.19) | copy-start | bytes 786436
  125.0 54.6 %copy-start.4 = (f32[2048]{0:T(1024)S(1)}, f32[2048]{0:T(1024)}, u32[]{:S(2)}) copy-start(f32[2048]{0:T(1024)} %param.30) | copy-start | bytes 24580
  179.4 6.1 %copy-start.2 = (bf16[64,2048]{1,0:T(8,128)(2,1)}, bf16[64,2048]{1,0:T(8,128)(2,1)S(1)}, u32[]{:S(2)}) copy-start(bf16[64,2048]{1,0:T(8,128)(2,1)S(1)} %reduce_sum.97) | copy-start | bytes 786436
  313.8 5.7 %copy-start.6 = (f32[64,8]{0,1:T(8,128)S(1)}, f32[64,8]{0,1:T(8,128)}, u32[]{:S(2)}) copy-start(f32[64,8]{0,1:T(8,128)} %param.32) | copy-start | bytes 6148
  313.8 81.2 %all-to-all-start.3 = ((bf16[128,192,128]{2,1,0:T(8,128)(2,1)}), bf16[128,192,128]{2,1,0:T(8,128)(2,1)}, u32[]{:S(2)}, u32[]{:S(2)}) async-start(bf16[128,192,128]{2,1,0:T(8,128)(2,1)} %reshape.327), calls=%async_computation.3 | async-start | bytes 12582912 | tf_op jit(solution)/shard_map/all_to_all | solution.py:163
